TPU v7x, 256 devices: a whole 4x4x8 slice. The times are simulated.
256 devices in a mesh: kv: 8 (over y, z_lo), blk: 32 (over x, z_hi, core).
Axes of the slice: x: 4, y: 4, z: 8 (z_hi: 4, z_lo: 2; z = z_hi * 2 + z_lo), core: 2. Of those that a mesh axis runs over, the one named last changes fastest.
Arguments:
- suffix_query: bfloat16 [6144, 4096], P('blk', 'kv'), may hold values from -6 to 6
- suffix_key_value: bfloat16 [2, 6144, 2048], P(None, 'blk', 'kv'), may hold values from -6 to 6
- suffix_resid: bfloat16 [6144, 4608], P('blk', 'kv'), may hold values from -6 to 6
- decode_query_rows: bfloat16 [64, 4096], P('blk', 'kv'), may hold values from -6 to 6
- decode_key_value: bfloat16 [2, 64, 2048], P(None, 'blk', 'kv'), may hold values from -6 to 6
- decode_resid: bfloat16 [64, 4608], P('blk', 'kv'), may hold values from -6 to 6
- out_weight: bfloat16 [4096, 4608], P('kv'), may hold values from -1.125 to 1.125
- post_gain: float32 [4608], P('kv'), may hold values from 0.1 to 1.9
- prefix_page_store: bfloat16 [2, 96, 128, 2048], P(None, 'blk', None, 'kv'), may hold values from -6 to 6
- prefix_table: int32 [96], replicated, may hold values from 0 to 95, each once
- decode_page_store: bfloat16 [2, 512, 128, 2048], P(None, 'blk', None, 'kv'), may hold values from -6 to 6
- page_table: int32 [512], replicated, may hold values from 0 to 511, each once
- suffix_lengths: int32 [16], replicated, may hold values from 1 to 768, 6144 in all
- suffix_prefix: int32 [16], replicated, may hold values from 0 to 3
- decode_ages: int32 [64], replicated, may hold values from 1 to 1023, as said below
Outputs:
- suffix_hidden: bfloat16 [6144, 4608], P('blk', 'kv')
- decode_hidden: bfloat16 [64, 4608], P('blk', 'kv')
- new_cache: bfloat16 [2, 512, 128, 2048], P(None, 'blk', None, 'kv')
Inputs may be any that keep to these rules, and one draw needn't show every extreme that they name: `page_table`: every page of the decode pool is named once. `prefix_table`: every page of the prefix pool is named once. `suffix_lengths`: the lengths sum to 6144; one is exactly 768. `decode_ages`: some slot has age 1024 - 1.
All inputs are finite; a program needn't handle non-finite values.
Results may differ from a plain program's by a relative error of at most 0.024.
Values may be sent and summed in bfloat16 or wider, within the bound.
No kernel may reach another device: no remote copies, remote signals or barrier semaphores. Data moves between devices by JAX's collectives and lax.ppermute only.
A program may use at most 128 MiB of HBM per device.

v0:
```python
import math
import jax
import jax.numpy as jnp
from jax import lax
from jax.sharding import PartitionSpec as P

D = 4608
QUERY_HEADS = 32
HEAD_SIZE = 128
PAGE_TOKENS = 128
PREFIX_LENGTH = 3072
SLOT_CAPACITY = 1024
soft_cap = 50.0
norm_eps = 1e-06


def from_behind(block, axis, distance):
    devices = range(lax.axis_size(axis))
    route = [(i - distance, i) for i in devices if i - distance in devices]
    return lax.ppermute(block, axis, route)


def attend(query_rows, key_rows, value_rows, visible, q_scale):
    logits = (
        jnp.einsum("qhgd,khd->qhgk", query_rows, key_rows, preferred_element_type=jnp.float32)
        * q_scale
    )
    capped = soft_cap * jnp.tanh(logits / soft_cap)
    weights = jnp.where(visible[:, None, None, :], jnp.exp(capped), 0.0)
    denominator = jnp.sum(weights, axis=3)
    numerator = jnp.einsum(
        "qhgk,khd->qhgd",
        weights.astype(jnp.bfloat16),
        value_rows,
        preferred_element_type=jnp.float32,
    )
    return (numerator, denominator)


def earlier(block_rows):
    return from_behind(block_rows, "blk", 1)


def token_tables(lengths, prefix_ids, token_ids):
    suffix_ends = jnp.cumsum(lengths)
    starts = suffix_ends - lengths
    inside = (
        (token_ids[:, None] >= starts[None, :]) & (token_ids[:, None] < suffix_ends[None, :])
    ).astype(jnp.int32)
    tok_start = jnp.sum(inside * starts[None, :], axis=1)
    tok_prefix = jnp.sum(inside * prefix_ids[None, :], axis=1)
    return (tok_start, tok_prefix)


def inverse_rows(table, wanted):
    hits = (table[None, :] == wanted[:, None]).astype(jnp.int32)
    places = jnp.arange(table.shape[0], dtype=jnp.int32)
    return jnp.sum(hits * places[None, :], axis=1)


def body(
    suffix_query,
    suffix_key_value,
    suffix_resid,
    decode_query_rows,
    decode_key_value,
    decode_resid,
    out_weight,
    post_gain,
    prefix_page_store,
    prefix_table,
    decode_page_store,
    page_table,
    suffix_lengths,
    suffix_prefix,
    decode_ages,
):
    head_dim = HEAD_SIZE
    page_len = PAGE_TOKENS
    q_scale = (D // QUERY_HEADS) ** (-0.5)
    tok_rows = suffix_query.shape[0]
    q_heads = suffix_query.shape[1] // head_dim
    kv_heads = suffix_key_value.shape[2] // head_dim
    query_group_width = q_heads // kv_heads
    my_index = lax.axis_index("blk")
    own_queries = suffix_query.reshape(tok_rows, kv_heads, query_group_width, head_dim)
    token_ids = my_index * tok_rows + jnp.arange(tok_rows, dtype=jnp.int32)
    tok_start, tok_prefix = token_tables(suffix_lengths, suffix_prefix, token_ids)
    look_back = 4
    pieces_back = [suffix_key_value]
    for step in range(look_back):
        pieces_back.insert(0, earlier(pieces_back[0]))
    window = jnp.concatenate(pieces_back, axis=1)
    key_ids = (my_index - look_back) * tok_rows + jnp.arange(
        (look_back + 1) * tok_rows, dtype=jnp.int32
    )
    visible = (key_ids[None, :] >= tok_start[:, None]) & (key_ids[None, :] <= token_ids[:, None])
    window_keys = window[0].reshape((look_back + 1) * tok_rows, kv_heads, head_dim)
    window_values = window[1].reshape((look_back + 1) * tok_rows, kv_heads, head_dim)
    own_numer, own_denom = attend(own_queries, window_keys, window_values, visible, q_scale)
    pool_pages = prefix_table.shape[0]
    page_owner = inverse_rows(prefix_table, jnp.arange(pool_pages, dtype=jnp.int32)) // (
        PREFIX_LENGTH // PAGE_TOKENS
    )
    all_queries = lax.all_gather(suffix_query, "blk", axis=0, tiled=True)
    all_tokens = all_queries.shape[0]
    all_ids = jnp.arange(all_tokens, dtype=jnp.int32)
    unused_start, all_prefix = token_tables(suffix_lengths, suffix_prefix, all_ids)
    local_pages = prefix_page_store.shape[1]
    held_owner = lax.dynamic_slice_in_dim(page_owner, my_index * local_pages, local_pages, 0)
    held_cols = jnp.repeat(held_owner, page_len)
    held_keys = prefix_page_store[0].reshape(local_pages * page_len, kv_heads, head_dim)
    held_values = prefix_page_store[1].reshape(local_pages * page_len, kv_heads, head_dim)
    block_rows = math.gcd(all_tokens, 1024)
    query_blocks = all_queries.reshape(
        all_tokens // block_rows, block_rows, kv_heads, query_group_width, head_dim
    )
    prefix_blocks = all_prefix.reshape(all_tokens // block_rows, block_rows)

    def one_block(element):
        block_queries, block_prefix = element
        seen = block_prefix[:, None] == held_cols[None, :]
        return attend(block_queries, held_keys, held_values, seen, q_scale)

    numer_all, denom_all = lax.map(one_block, (query_blocks, prefix_blocks))
    numer_all = numer_all.reshape(all_tokens, kv_heads, query_group_width, head_dim)
    denom_all = denom_all.reshape(all_tokens, kv_heads, query_group_width)
    pre_numer, pre_denom = (
        lax.psum_scatter(
            numer_all.astype(jnp.bfloat16), "blk", scatter_dimension=0, tiled=True
        ).astype(jnp.float32),
        lax.psum_scatter(
            denom_all.astype(jnp.bfloat16), "blk", scatter_dimension=0, tiled=True
        ).astype(jnp.float32),
    )
    suffix_attn = ((own_numer + pre_numer) / (own_denom + pre_denom)[..., None]).astype(
        jnp.bfloat16
    )
    suffix_attn = suffix_attn.reshape(tok_rows, q_heads * head_dim)
    all_dq, all_dkv = (
        lax.all_gather(decode_query_rows, "blk", axis=0, tiled=True),
        lax.all_gather(decode_key_value, "blk", axis=1, tiled=True),
    )
    slot_total = all_dq.shape[0]
    slot_pages = SLOT_CAPACITY // PAGE_TOKENS
    local_cache = decode_page_store.shape[1]
    page_ids = my_index * local_cache + jnp.arange(local_cache, dtype=jnp.int32)
    position = inverse_rows(page_table, page_ids)
    slot_of = position // slot_pages
    block_of = position % slot_pages
    slot_hot = slot_of[:, None] == jnp.arange(slot_total, dtype=jnp.int32)[None, :]
    page_age = jnp.sum(slot_hot.astype(jnp.int32) * decode_ages[None, :], axis=1)
    select = slot_hot.astype(jnp.bfloat16)
    new_rows = jnp.einsum(
        "ls,tsc->tlc", select, all_dkv, preferred_element_type=jnp.float32
    ).astype(jnp.bfloat16)
    write_here = (block_of == page_age // page_len)[:, None] & (
        jnp.arange(page_len, dtype=jnp.int32)[None, :] == (page_age % page_len)[:, None]
    )
    new_cache = jnp.where(write_here[None, :, :, None], new_rows[:, :, None, :], decode_page_store)
    page_queries = jnp.dot(select, all_dq, preferred_element_type=jnp.float32).astype(jnp.bfloat16)
    page_queries = page_queries.reshape(local_cache, kv_heads, query_group_width, head_dim)
    key_cache = new_cache[0].reshape(local_cache, page_len, kv_heads, head_dim)
    value_cache = new_cache[1].reshape(local_cache, page_len, kv_heads, head_dim)
    logits = (
        jnp.einsum("lhgd,lphd->lhgp", page_queries, key_cache, preferred_element_type=jnp.float32)
        * q_scale
    )
    capped = soft_cap * jnp.tanh(logits / soft_cap)
    places = block_of[:, None] * page_len + jnp.arange(page_len, dtype=jnp.int32)[None, :]
    seen_pos = places <= page_age[:, None]
    weights = jnp.where(seen_pos[:, None, None, :], jnp.exp(capped), 0.0)
    page_denom = jnp.sum(weights, axis=3)
    page_numer = jnp.einsum(
        "lhgp,lphd->lhgd",
        weights.astype(jnp.bfloat16),
        value_cache,
        preferred_element_type=jnp.float32,
    )
    slot_float = slot_hot.astype(jnp.float32)
    slot_numer = jnp.einsum(
        "ls,lhgd->shgd", slot_float, page_numer, precision=lax.Precision.HIGHEST
    )
    slot_denom = jnp.einsum("ls,lhg->shg", slot_float, page_denom, precision=lax.Precision.HIGHEST)
    mine_numer, mine_denom = (
        lax.psum_scatter(
            slot_numer.astype(jnp.bfloat16), "blk", scatter_dimension=0, tiled=True
        ).astype(jnp.float32),
        lax.psum_scatter(
            slot_denom.astype(jnp.bfloat16), "blk", scatter_dimension=0, tiled=True
        ).astype(jnp.float32),
    )
    decode_attn = (mine_numer / mine_denom[..., None]).astype(jnp.bfloat16)
    decode_rows = decode_attn.shape[0]
    decode_attn = decode_attn.reshape(decode_rows, q_heads * head_dim)
    attention = jnp.concatenate([suffix_attn, decode_attn], axis=0)
    projected = jnp.dot(attention, out_weight, preferred_element_type=jnp.float32)
    residual = jnp.concatenate([suffix_resid, decode_resid], axis=0).astype(jnp.float32)
    mine = lax.psum_scatter(
        projected.astype(jnp.bfloat16), "kv", scatter_dimension=1, tiled=True
    ).astype(jnp.float32)
    mean_square = lax.psum(jnp.sum(mine * mine, axis=1), "kv") / D
    normed = mine * lax.rsqrt(mean_square + norm_eps)[:, None] * post_gain[None, :]
    hidden = (residual + normed).astype(jnp.bfloat16)
    return (hidden[:tok_rows], hidden[tok_rows:], new_cache)


def solution(mesh):
    placed = (
        P("blk", "kv"),
        P(None, "blk", "kv"),
        P("blk", "kv"),
        P("blk", "kv"),
        P(None, "blk", "kv"),
        P("blk", "kv"),
        P("kv", None),
        P("kv"),
        P(None, "blk", None, "kv"),
        P(),
        P(None, "blk", None, "kv"),
        P(),
        P(),
        P(),
        P(),
    )
    return jax.shard_map(
        body,
        mesh=mesh,
        in_specs=placed,
        out_specs=(P("blk", "kv"), P("blk", "kv"), P(None, "blk", None, "kv")),
        check_vma=False,
    )
```

profile of v0, /device:TPU:2, one launch (start us, length us, event | category | flops | bytes accessed | tf_op | source)
XLA Modules:
  0.0 656.7 jit_solution(15037850193555876869)
XLA Ops:
  7.2 0.7 all-gather.3.cloned.1.call-update
  8.0 0.7 copy.88
  8.7 3.9 copy.90
  12.6 42.1 %all-gather = bf16[32,2,512]{2,1,0:T(2,128)(2,1)S(1)} all-gather(bf16[1,2,512]{2,1,0:T(2,128)(2,1)S(1)} %bitcast.118), channel_id=1, replica_groups=mesh['kv'=8,'blk'=32] {'blk'}, dimensions={0}, use_global_device_ids=true | all-gather | bytes 67584 | tf_op jit(solution)/shard_map/all_gather | solution.py:141
  55.2 42.4 %all_gather.11 = bf16[2,64,256]{2,0,1:T(2,128)(2,1)S(1)} all-gather(bf16[2,2,256]{2,0,1:T(2,128)(2,1)S(1)} %copy.88), channel_id=1, replica_groups=mesh['kv'=8,'blk'=32] {'blk'}, dimensions={1}, use_global_device_ids=true | all-gather | bytes 67584 | tf_op jit(solution)/shard_map/all_gather | solution.py:142
  98.1 2.5 broadcast_select_fusion
  100.7 0.5 fusion.69
  101.2 0.6 fusion.47
  101.9 1.0 convolution_convert_fusion.1
  103.9 9.7 %reshape.292 = bf16[6,1024,2,2,128]{4,3,2,1,0:T(2,128)(2,1)} reshape(bf16[6144,512]{1,0:T(8,128)(2,1)} %all-gather.3.cloned.1.call-done) | data formatting | bytes 12582912 | tf_op jit(solution)/shard_map/reshape | solution.py:115
  113.6 49.5 %while.15 = (s32[]{:T(128)}, bf16[6,1024,2,2,128]{4,1,3,2,0:T(8,128)(2,1)}, bf16[6,1024,2,2]{1,3,2,0:T(2,128)(2,1)S(1)}, s32[6,1024]{1,0:T(8,128)S(1)}, bf16[6,1...) while((s32[]{:T(128)}, ...), condition=%wide.region_6.7_spmd.clone, body=%wide.region_4.6_spmd.clone.sunk | while | flops 818278400 | bytes 19439220 | solution.py:125
  113.7 0.3 broadcast_compare_fusion.2
  114.0 2.0 constant_dynamic-slice_fusion.5
  115.9 2.7 bitcast_reduce_fusion.2
  118.6 3.2 bitcast_dynamic-update-slice_fusion.4
  122.0 0.3 broadcast_compare_fusion.2
  122.2 2.0 constant_dynamic-slice_fusion.5
  124.2 2.7 bitcast_reduce_fusion.2
  126.9 3.2 bitcast_dynamic-update-slice_fusion.4
  130.2 0.3 broadcast_compare_fusion.2
  130.5 2.0 constant_dynamic-slice_fusion.5
  132.4 2.7 bitcast_reduce_fusion.2
  135.1 3.2 bitcast_dynamic-update-slice_fusion.4
  138.4 0.3 broadcast_compare_fusion.2
  138.7 2.0 constant_dynamic-slice_fusion.5
  140.6 2.7 bitcast_reduce_fusion.2
  143.3 3.2 bitcast_dynamic-update-slice_fusion.4
  146.6 0.3 broadcast_compare_fusion.2
  146.9 2.0 constant_dynamic-slice_fusion.5
  148.9 2.7 bitcast_reduce_fusion.2
  151.6 3.2 bitcast_dynamic-update-slice_fusion.4
  154.9 0.3 broadcast_compare_fusion.2
  155.2 2.0 constant_dynamic-slice_fusion.5
  157.1 2.7 bitcast_reduce_fusion.2
  159.8 3.2 bitcast_dynamic-update-slice_fusion.4
  163.1 5.8 copy.117
  168.9 6.3 reshape.304
  175.2 6.1 copy.85
  181.3 0.8 copy-done.3
  182.2 2.2 collective-permute-start
  184.5 0.6 dynamic-slice
  185.7 0.3 convolution_convert_fusion.2
  186.0 125.5 %all-reduce.1 = bf16[64,2,2]{2,0,1:T(8,128)(2,1)S(1)} all-reduce(bf16[64,2,2]{2,0,1:T(8,128)(2,1)S(1)} %convolution_convert_fusion.2), channel_id=5, replica_groups=mesh['kv'=8,'blk'=32] {'blk'}, use_global_device_ids=true, to_apply=%region_14.15.clone | all-reduce | flops 256 | bytes 1024
  311.7 1.9 collective-permute-start.1
  313.7 8.1 %collective-permute-done.1 = bf16[2,192,256]{2,1,0:T(8,128)(2,1)S(1)} collective-permute-done((bf16[2,192,256]{2,1,0:T(8,128)(2,1)S(1)}, bf16[2,192,256]{2,1,0:T(8,128)(2,1)S(1)}, u32[]{:S(2)}, u32[]{:S(2)}) %collective-permute-start.1) | collective-permute-done | bytes 196640 | tf_op jit(solution)/shard_map/ppermute | solution.py:20
  321.8 1.9 collective-permute-start.2
  323.9 7.8 %collective-permute-done.2 = bf16[2,192,256]{2,1,0:T(8,128)(2,1)S(1)} collective-permute-done((bf16[2,192,256]{2,1,0:T(8,128)(2,1)S(1)}, bf16[2,192,256]{2,1,0:T(8,128)(2,1)S(1)}, u32[]{:S(2)}, u32[]{:S(2)}) %collective-permute-start.2) | collective-permute-done | bytes 196640 | tf_op jit(solution)/shard_map/ppermute | solution.py:20
  331.8 2.1 collective-permute-start.3
  333.9 9.5 %all-reduce.4.cloned.1.call-done = bf16[64,2,2,128]{3,0,2,1:T(8,128)(2,1)} async-done(((bf16[64,2,2,128]{3,0,2,1:T(8,128)(2,1)}), bf16[64,2,2,128]{3,0,2,1:T(8,128)(2,1)}) %all-reduce.4.cloned.1.call-update) | async-done | bytes 65552
  343.4 0.8 fusion.56
  344.3 0.9 reshape_squeeze.19
  345.4 3.9 fusion.10
  349.2 99.7 %reduce-scatter.12.cloned.1.call-done = bf16[192,4]{1,0:T(8,128)(2,1)} async-done(((bf16[6144,4]{1,0:T(8,128)(2,1)}), bf16[192,4]{1,0:T(8,128)(2,1)}) %reduce-scatter.12.cloned.1.call-update) | async-done | bytes 1552
  448.9 0.9 reshape.305
  449.9 109.7 %reduce-scatter.10.cloned.1.call-done = bf16[192,2,2,128]{3,0,2,1:T(8,128)(2,1)} async-done(((bf16[6144,2,2,128]{3,0,2,1:T(8,128)(2,1)}), bf16[192,2,2,128]{3,0,2,1:T(8,128)(2,1)}) %reduce-scatter.10.cloned.1.call-update) | async-done | bytes 196624 | tf_op jit(solution)/shard_map/reduce_scatter | solution.py:129
  559.6 2.9 fusion.29
  562.8 4.7 convolution_convert_fusion
  567.5 4.0 copy.115
  571.6 2.6 copy.96
  574.2 56.4 %reduce-scatter.14.cloned.1.call-done = bf16[576,194]{1,0:T(8,128)(2,1)} async-done(((bf16[4608,194]{1,0:T(8,128)(2,1)}), bf16[576,194]{1,0:T(8,128)(2,1)}) %reduce-scatter.14.cloned.1.call-update) | async-done | bytes 223504
  630.5 1.1 copy.116
  631.8 16.9 %psum.7 = f32[194]{0:T(256)S(1)} all-reduce(f32[194]{0:T(256)S(1)} %fusion.32), channel_id=1, replica_groups=mesh['kv'=8,'blk'=32] {'kv'}, use_global_device_ids=true, to_apply=%region_17.18 | all-reduce | flops 194 | bytes 1552 | tf_op jit(solution)/shard_map/psum | solution.py:202
  648.9 0.7 slice.36
  649.6 0.6 slice.37
  (106 shorter events, 4.3 us)
Async XLA Ops:
  7.2 5.4 copy-start.6
  7.2 47.6 %copy-start.7 = (s32[512]{0:T(512)S(1)}, s32[512]{0:T(512)}, u32[]{:S(2)}) copy-start(s32[512]{0:T(512)} %param.28) | copy-start | bytes 6148
  7.2 90.3 %copy-start.10 = (s32[64]{0:T(128)S(1)}, s32[64]{0:T(128)}, u32[]{:S(2)}) copy-start(s32[64]{0:T(128)} %param.31) | copy-start | bytes 772
  7.2 96.7 %all-gather.3.cloned.1.call-start = ((), (), s32[]{:S(2)}) async-start(), calls=%async_computation.3 | async-start | bytes 6488064 | tf_op jit(solution)/shard_map/all_gather | solution.py:105
  7.9 335.4 %all-reduce.4.cloned.1.call-start = ((), (), s32[]{:S(2)}) async-start(), calls=%async_computation.7 | async-start | bytes 131072
  100.6 2.4 copy-start.11
  100.6 2.5 copy-start.8
  100.6 2.8 copy-start.9
  100.6 3.0 copy-start.1
  102.9 346.0 %reduce-scatter.12.cloned.1.call-start = ((), (), s32[]{:S(2)}) async-start(), calls=%async_computation.5 | async-start | bytes 1622016
  175.1 384.5 %reduce-scatter.10.cloned.1.call-start = ((), (), s32[]{:S(2)}) async-start(), calls=%async_computation.4 | async-start | bytes 6488064 | tf_op jit(solution)/shard_map/reduce_scatter | solution.py:129
  181.2 0.9 copy-start.3
  181.2 3.2 copy-start
  181.2 3.3 copy-start.12
  181.3 449.3 %reduce-scatter.14.cloned.1.call-start = ((), (), s32[]{:S(2)}) async-start(), calls=%async_computation.6 | async-start | bytes 2654208
  182.2 129.5 %collective-permute-start = (bf16[2,192,256]{2,1,0:T(8,128)(2,1)S(1)}, bf16[2,192,256]{2,1,0:T(8,128)(2,1)S(1)}, u32[]{:S(2)}, u32[]{:S(2)}) collective-permute-start(bf16[2,192,256]{2,1,0:T(8,128)(2,1)S(1)} %copy-done.3), channel_id=1, source_target_pairs={{0,1},{1,2},{2,3},{3,4},{4,5},{5,6},{6,7},{7,8},{8,9},{9,10},{10,1... | collective-permute-start | bytes 589832 | tf_op jit(solution)/shard_map/ppermute | solution.py:20
  311.7 10.1 %collective-permute-start.1 = (bf16[2,192,256]{2,1,0:T(8,128)(2,1)S(1)}, bf16[2,192,256]{2,1,0:T(8,128)(2,1)S(1)}, u32[]{:S(2)}, u32[]{:S(2)}) collective-permute-start(bf16[2,192,256]{2,1,0:T(8,128)(2,1)S(1)} %collective-permute-done), channel_id=1, source_target_pairs={{0,1},{1,2},{2,3},{3,4},{4,5},{5,6},{6,7},{7,8},{8,9},{9,10},{10,1... | collective-permute-start | bytes 589832 | tf_op jit(solution)/shard_map/ppermute | solution.py:20
  321.8 10.0 %collective-permute-start.2 = (bf16[2,192,256]{2,1,0:T(8,128)(2,1)S(1)}, bf16[2,192,256]{2,1,0:T(8,128)(2,1)S(1)}, u32[]{:S(2)}, u32[]{:S(2)}) collective-permute-start(bf16[2,192,256]{2,1,0:T(8,128)(2,1)S(1)} %collective-permute-done.1), channel_id=1, source_target_pairs={{0,1},{1,2},{2,3},{3,4},{4,5},{5,6},{6,7},{7,8},{8,9},{9,10},{10,1... | collective-permute-start | bytes 589832 | tf_op jit(solution)/shard_map/ppermute | solution.py:20
  331.8 12.4 %collective-permute-start.3 = (bf16[2,192,256]{2,1,0:T(8,128)(2,1)S(1)}, bf16[2,192,256]{2,1,0:T(8,128)(2,1)S(1)}, u32[]{:S(2)}, u32[]{:S(2)}) collective-permute-start(bf16[2,192,256]{2,1,0:T(8,128)(2,1)S(1)} %collective-permute-done.2), channel_id=1, source_target_pairs={{0,1},{1,2},{2,3},{3,4},{4,5},{5,6},{6,7},{7,8},{8,9},{9,10},{10,1... | collective-permute-start | bytes 589832 | tf_op jit(solution)/shard_map/ppermute | solution.py:20
  571.5 77.2 %copy-start.2 = (bf16[192,576]{1,0:T(8,128)(2,1)S(1)}, bf16[192,576]{1,0:T(8,128)(2,1)}, u32[]{:S(2)}) copy-start(bf16[192,576]{1,0:T(8,128)(2,1)} %param.19) | copy-start | bytes 663556
  571.5 77.2 %copy-start.4 = (f32[576]{0:T(1024)S(1)}, f32[576]{0:T(1024)}, u32[]{:S(2)}) copy-start(f32[576]{0:T(1024)} %param.24) | copy-start | bytes 6916
  571.6 77.2 %copy-start.5 = (bf16[2,576]{1,0:T(2,128)(2,1)S(1)}, bf16[2,576]{1,0:T(2,128)(2,1)}, u32[]{:S(2)}) copy-start(bf16[2,576]{1,0:T(2,128)(2,1)} %param.22) | copy-start | bytes 6916
Sparse Core Ops, SparseCore 0:
  10.5 72.2 all-gather.2
  103.0 240.3 all-reduce.3
  347.8 101.0 reduce-scatter.11
  452.8 106.7 reduce-scatter.9
  571.7 58.8 reduce-scatter.13
where the time goes:
time: 658 us; the launch traced here: 657 us
  waiting for transfers between devices  292 us (44%)
  blocking collectives  227 us (34%)
  local copies, waits for them, and re-layouts  58.4 us (9%)
  matrix products  49.5 us (8%)
  between operations  14.8 us (2%)
  starting transfers between devices  8.36 us (1%)
  other arithmetic  6.68 us (1%)
    unnamed x8, waiting for transfers between devices  166 us
    unnamed x1, blocking collectives  126 us
    reduce_scatter x1, waiting for transfers between devices, body(): lax.psum_scatter(numer_all.astype(jnp.bfloat16), 'blk', scatter_dimension...  110 us
    all_gather x1, blocking collectives, body(): lax.all_gather(decode_key_value, 'blk', axis=1, tiled=True)  42.4 us
    all_gather x1, blocking collectives, body(): lax.all_gather(decode_query_rows, 'blk', axis=0, tiled=True)  42.1 us
    unnamed x43, local copies, waits for them, and re-layouts  27.1 us
    dot_general x7, matrix products, attend(): jnp.einsum('qhgk,khd->qhgd', weights.astype(jnp.bfloat16), value_rows, pr...  22.1 us
    dot_general x7, matrix products, attend(): jnp.einsum('qhgd,khd->qhgk', query_rows, key_rows, preferred_element_type...  19.9 us
  transfers between devices with their start and end apart: 9, of which 6 were waited for; matrix products, arithmetic and copies ran while one was open for 15% of the time, Pallas kernels for 0%

commit v1 on v0

--- a/solution.py
+++ b/solution.py
@@ -199,7 +199,7 @@
     mine = lax.psum_scatter(
         projected.astype(jnp.bfloat16), "kv", scatter_dimension=1, tiled=True
     ).astype(jnp.float32)
-    mean_square = lax.psum(jnp.sum(mine * mine, axis=1), "kv") / D
+    mean_square = jnp.sum(lax.all_gather(jnp.sum(mine * mine, axis=1), "kv"), axis=0) / D
     normed = mine * lax.rsqrt(mean_square + norm_eps)[:, None] * post_gain[None, :]
     hidden = (residual + normed).astype(jnp.bfloat16)
     return (hidden[:tok_rows], hidden[tok_rows:], new_cache)

time: 658 us -> 659 us (level)
    unnamed x1 -> x2, blocking collectives: 126 us -> 143 us
    psum x1 -> x0, blocking collectives: 16.9 us -> none  [body(): mean_square = lax.psum(jnp.sum(mine * mine, axis=1), 'kv') / D]
    unnamed x43 -> x48, local copies, waits for them, and re-layouts: 27.1 us -> 27.9 us
where the time goes in v1:
time: 659 us; the launch traced here: 657 us
  waiting for transfers between devices  291 us (44%)
  blocking collectives  227 us (34%)
  local copies, waits for them, and re-layouts  59.4 us (9%)
  matrix products  49.5 us (8%)
  between operations  15.5 us (2%)
  starting transfers between devices  8.35 us (1%)
  other arithmetic  6.7 us (1%)
    unnamed x8, waiting for transfers between devices  165 us
    unnamed x2, blocking collectives  143 us
    reduce_scatter x1, waiting for transfers between devices, body(): lax.psum_scatter(numer_all.astype(jnp.bfloat16), 'blk', scatter_dimension...  110 us
    all_gather x1, blocking collectives, body(): lax.all_gather(decode_key_value, 'blk', axis=1, tiled=True)  42.4 us
    all_gather x1, blocking collectives, body(): lax.all_gather(decode_query_rows, 'blk', axis=0, tiled=True)  42.1 us
    unnamed x48, local copies, waits for them, and re-layouts  27.9 us
    dot_general x7, matrix products, attend(): jnp.einsum('qhgk,khd->qhgd', weights.astype(jnp.bfloat16), value_rows, pr...  22.1 us
    dot_general x7, matrix products, attend(): jnp.einsum('qhgd,khd->qhgk', query_rows, key_rows, preferred_element_type...  19.9 us
  transfers between devices with their start and end apart: 9, of which 6 were waited for; matrix products, arithmetic and copies ran while one was open for 15% of the time, Pallas kernels for 0%

profile of v1, /device:TPU:2, one launch (start us, length us, event | category | flops | bytes accessed | tf_op | source)
XLA Modules:
  0.0 657.4 jit_solution(17358115041359551645)
XLA Ops:
  7.2 0.7 all-gather.4.cloned.1.call-update
  8.0 0.7 copy.88
  8.7 3.9 copy.90
  12.6 42.1 %all-gather.1 = bf16[32,2,512]{2,1,0:T(2,128)(2,1)S(1)} all-gather(bf16[1,2,512]{2,1,0:T(2,128)(2,1)S(1)} %bitcast.119), channel_id=1, replica_groups=mesh['kv'=8,'blk'=32] {'blk'}, dimensions={0}, use_global_device_ids=true | all-gather | bytes 67584 | tf_op jit(solution)/shard_map/all_gather | solution.py:141
  55.2 42.4 %all_gather.17 = bf16[2,64,256]{2,0,1:T(2,128)(2,1)S(1)} all-gather(bf16[2,2,256]{2,0,1:T(2,128)(2,1)S(1)} %copy.88), channel_id=1, replica_groups=mesh['kv'=8,'blk'=32] {'blk'}, dimensions={1}, use_global_device_ids=true | all-gather | bytes 67584 | tf_op jit(solution)/shard_map/all_gather | solution.py:142
  98.1 2.5 broadcast_select_fusion
  100.8 0.5 fusion.69
  101.2 0.6 fusion.47
  101.9 1.0 convolution_convert_fusion.1
  103.9 9.7 %reshape.296 = bf16[6,1024,2,2,128]{4,3,2,1,0:T(2,128)(2,1)} reshape(bf16[6144,512]{1,0:T(8,128)(2,1)} %all-gather.4.cloned.1.call-done) | data formatting | bytes 12582912 | tf_op jit(solution)/shard_map/reshape | solution.py:115
  113.6 49.5 %while.15 = (s32[]{:T(128)}, bf16[6,1024,2,2,128]{4,1,3,2,0:T(8,128)(2,1)}, bf16[6,1024,2,2]{1,3,2,0:T(2,128)(2,1)S(1)}, s32[6,1024]{1,0:T(8,128)S(1)}, bf16[6,1...) while((s32[]{:T(128)}, ...), condition=%wide.region_6.7_spmd.clone, body=%wide.region_4.6_spmd.clone.sunk | while | flops 818278400 | bytes 19439220 | solution.py:125
  113.7 0.3 broadcast_compare_fusion.2
  114.0 2.0 constant_dynamic-slice_fusion.5
  115.9 2.7 bitcast_reduce_fusion.2
  118.6 3.2 bitcast_dynamic-update-slice_fusion.4
  122.0 0.3 broadcast_compare_fusion.2
  122.3 2.0 constant_dynamic-slice_fusion.5
  124.2 2.7 bitcast_reduce_fusion.2
  126.9 3.2 bitcast_dynamic-update-slice_fusion.4
  130.2 0.3 broadcast_compare_fusion.2
  130.5 2.0 constant_dynamic-slice_fusion.5
  132.4 2.7 bitcast_reduce_fusion.2
  135.1 3.2 bitcast_dynamic-update-slice_fusion.4
  138.4 0.3 broadcast_compare_fusion.2
  138.7 2.0 constant_dynamic-slice_fusion.5
  140.7 2.7 bitcast_reduce_fusion.2
  143.3 3.2 bitcast_dynamic-update-slice_fusion.4
  146.6 0.3 broadcast_compare_fusion.2
  146.9 2.0 constant_dynamic-slice_fusion.5
  148.9 2.7 bitcast_reduce_fusion.2
  151.6 3.2 bitcast_dynamic-update-slice_fusion.4
  155.2 2.0 constant_dynamic-slice_fusion.5
  157.1 2.7 bitcast_reduce_fusion.2
  159.8 3.2 bitcast_dynamic-update-slice_fusion.4
  163.1 5.8 copy.117
  168.9 6.3 reshape.314
  175.2 6.1 copy.85
  181.3 0.8 copy-done.3
  182.2 2.2 collective-permute-start
  184.5 0.6 dynamic-slice.1
  185.7 0.3 convolution_convert_fusion.2
  186.0 125.4 %all-reduce.2 = bf16[64,2,2]{2,0,1:T(8,128)(2,1)S(1)} all-reduce(bf16[64,2,2]{2,0,1:T(8,128)(2,1)S(1)} %convolution_convert_fusion.2), channel_id=6, replica_groups=mesh['kv'=8,'blk'=32] {'blk'}, use_global_device_ids=true, to_apply=%region_14.15.clone | all-reduce | flops 256 | bytes 1024
  311.6 1.9 collective-permute-start.1
  313.6 8.1 %collective-permute-done.1 = bf16[2,192,256]{2,1,0:T(8,128)(2,1)S(1)} collective-permute-done((bf16[2,192,256]{2,1,0:T(8,128)(2,1)S(1)}, bf16[2,192,256]{2,1,0:T(8,128)(2,1)S(1)}, u32[]{:S(2)}, u32[]{:S(2)}) %collective-permute-start.1) | collective-permute-done | bytes 196640 | tf_op jit(solution)/shard_map/ppermute | solution.py:20
  321.7 1.9 collective-permute-start.2
  323.9 7.8 %collective-permute-done.2 = bf16[2,192,256]{2,1,0:T(8,128)(2,1)S(1)} collective-permute-done((bf16[2,192,256]{2,1,0:T(8,128)(2,1)S(1)}, bf16[2,192,256]{2,1,0:T(8,128)(2,1)S(1)}, u32[]{:S(2)}, u32[]{:S(2)}) %collective-permute-start.2) | collective-permute-done | bytes 196640 | tf_op jit(solution)/shard_map/ppermute | solution.py:20
  331.7 2.1 collective-permute-start.3
  333.8 9.6 %all-reduce.5.cloned.1.call-done = bf16[64,2,2,128]{3,0,2,1:T(8,128)(2,1)} async-done(((bf16[64,2,2,128]{3,0,2,1:T(8,128)(2,1)}), bf16[64,2,2,128]{3,0,2,1:T(8,128)(2,1)}) %all-reduce.5.cloned.1.call-update) | async-done | bytes 65552
  343.4 0.8 fusion.56
  344.4 0.9 reshape_squeeze.19
  345.4 3.9 fusion.10
  349.3 99.7 %reduce-scatter.12.cloned.1.call-done = bf16[192,4]{1,0:T(8,128)(2,1)} async-done(((bf16[6144,4]{1,0:T(8,128)(2,1)}), bf16[192,4]{1,0:T(8,128)(2,1)}) %reduce-scatter.12.cloned.1.call-update) | async-done | bytes 1552
  448.9 0.9 reshape.315
  449.9 109.7 %reduce-scatter.10.cloned.1.call-done = bf16[192,2,2,128]{3,0,2,1:T(8,128)(2,1)} async-done(((bf16[6144,2,2,128]{3,0,2,1:T(8,128)(2,1)}), bf16[192,2,2,128]{3,0,2,1:T(8,128)(2,1)}) %reduce-scatter.10.cloned.1.call-update) | async-done | bytes 196624 | tf_op jit(solution)/shard_map/reduce_scatter | solution.py:129
  559.6 2.9 fusion.29
  562.8 4.7 convolution_convert_fusion
  567.5 4.0 copy.115
  571.6 2.6 copy.96
  574.2 0.6 dynamic-slice
  575.4 55.1 %reduce-scatter.14.cloned.1.call-done = bf16[576,194]{1,0:T(8,128)(2,1)} async-done(((bf16[4608,194]{1,0:T(8,128)(2,1)}), bf16[576,194]{1,0:T(8,128)(2,1)}) %reduce-scatter.14.cloned.1.call-update) | async-done | bytes 223504
  630.5 1.1 copy.116
  632.1 17.2 %all-reduce = f32[1552]{0:T(1024)S(1)} all-reduce(f32[1552]{0:T(1024)S(1)} %dynamic-update-slice), channel_id=2, replica_groups=mesh['kv'=8,'blk'=32] {'kv'}, use_global_device_ids=true, to_apply=%add | all-reduce | flops 1552 | bytes 12416
  649.6 0.7 slice.36
  650.3 0.6 slice.37
  (113 shorter events, 5.0 us)
Async XLA Ops:
  7.2 5.4 copy-start.6
  7.2 47.6 %copy-start.7 = (s32[512]{0:T(512)S(1)}, s32[512]{0:T(512)}, u32[]{:S(2)}) copy-start(s32[512]{0:T(512)} %param.28) | copy-start | bytes 6148
  7.2 90.3 %copy-start.10 = (s32[64]{0:T(128)S(1)}, s32[64]{0:T(128)}, u32[]{:S(2)}) copy-start(s32[64]{0:T(128)} %param.31) | copy-start | bytes 772
  7.2 96.7 %all-gather.4.cloned.1.call-start = ((), (), s32[]{:S(2)}) async-start(), calls=%async_computation.3 | async-start | bytes 6488064 | tf_op jit(solution)/shard_map/all_gather | solution.py:105
  7.9 335.5 %all-reduce.5.cloned.1.call-start = ((), (), s32[]{:S(2)}) async-start(), calls=%async_computation.7 | async-start | bytes 131072
  100.6 2.4 copy-start.11
  100.6 2.5 copy-start.8
  100.6 2.8 copy-start.9
  100.6 3.0 copy-start.1
  102.9 346.0 %reduce-scatter.12.cloned.1.call-start = ((), (), s32[]{:S(2)}) async-start(), calls=%async_computation.5 | async-start | bytes 1622016
  175.2 384.4 %reduce-scatter.10.cloned.1.call-start = ((), (), s32[]{:S(2)}) async-start(), calls=%async_computation.4 | async-start | bytes 6488064 | tf_op jit(solution)/shard_map/reduce_scatter | solution.py:129
  181.3 0.9 copy-start.3
  181.3 3.2 copy-start
  181.3 3.2 copy-start.13
  181.3 449.2 %reduce-scatter.14.cloned.1.call-start = ((), (), s32[]{:S(2)}) async-start(), calls=%async_computation.6 | async-start | bytes 2654208
  182.2 129.4 %collective-permute-start = (bf16[2,192,256]{2,1,0:T(8,128)(2,1)S(1)}, bf16[2,192,256]{2,1,0:T(8,128)(2,1)S(1)}, u32[]{:S(2)}, u32[]{:S(2)}) collective-permute-start(bf16[2,192,256]{2,1,0:T(8,128)(2,1)S(1)} %copy-done.3), channel_id=1, source_target_pairs={{0,1},{1,2},{2,3},{3,4},{4,5},{5,6},{6,7},{7,8},{8,9},{9,10},{10,1... | collective-permute-start | bytes 589832 | tf_op jit(solution)/shard_map/ppermute | solution.py:20
  311.6 10.1 %collective-permute-start.1 = (bf16[2,192,256]{2,1,0:T(8,128)(2,1)S(1)}, bf16[2,192,256]{2,1,0:T(8,128)(2,1)S(1)}, u32[]{:S(2)}, u32[]{:S(2)}) collective-permute-start(bf16[2,192,256]{2,1,0:T(8,128)(2,1)S(1)} %collective-permute-done), channel_id=1, source_target_pairs={{0,1},{1,2},{2,3},{3,4},{4,5},{5,6},{6,7},{7,8},{8,9},{9,10},{10,1... | collective-permute-start | bytes 589832 | tf_op jit(solution)/shard_map/ppermute | solution.py:20
  321.7 10.0 %collective-permute-start.2 = (bf16[2,192,256]{2,1,0:T(8,128)(2,1)S(1)}, bf16[2,192,256]{2,1,0:T(8,128)(2,1)S(1)}, u32[]{:S(2)}, u32[]{:S(2)}) collective-permute-start(bf16[2,192,256]{2,1,0:T(8,128)(2,1)S(1)} %collective-permute-done.1), channel_id=1, source_target_pairs={{0,1},{1,2},{2,3},{3,4},{4,5},{5,6},{6,7},{7,8},{8,9},{9,10},{10,1... | collective-permute-start | bytes 589832 | tf_op jit(solution)/shard_map/ppermute | solution.py:20
  331.7 12.5 %collective-permute-start.3 = (bf16[2,192,256]{2,1,0:T(8,128)(2,1)S(1)}, bf16[2,192,256]{2,1,0:T(8,128)(2,1)S(1)}, u32[]{:S(2)}, u32[]{:S(2)}) collective-permute-start(bf16[2,192,256]{2,1,0:T(8,128)(2,1)S(1)} %collective-permute-done.2), channel_id=1, source_target_pairs={{0,1},{1,2},{2,3},{3,4},{4,5},{5,6},{6,7},{7,8},{8,9},{9,10},{10,1... | collective-permute-start | bytes 589832 | tf_op jit(solution)/shard_map/ppermute | solution.py:20
  571.5 2.6 copy-start.12
  571.5 77.9 %copy-start.2 = (bf16[192,576]{1,0:T(8,128)(2,1)S(1)}, bf16[192,576]{1,0:T(8,128)(2,1)}, u32[]{:S(2)}) copy-start(bf16[192,576]{1,0:T(8,128)(2,1)} %param.19) | copy-start | bytes 663556
  571.5 77.9 %copy-start.4 = (f32[576]{0:T(1024)S(1)}, f32[576]{0:T(1024)}, u32[]{:S(2)}) copy-start(f32[576]{0:T(1024)} %param.24) | copy-start | bytes 6916
  571.5 77.9 %copy-start.5 = (bf16[2,576]{1,0:T(2,128)(2,1)S(1)}, bf16[2,576]{1,0:T(2,128)(2,1)}, u32[]{:S(2)}) copy-start(bf16[2,576]{1,0:T(2,128)(2,1)} %param.22) | copy-start | bytes 6916
Sparse Core Ops, SparseCore 0:
  10.5 72.2 all-gather.3
  103.0 240.3 all-reduce.4
  347.8 101.0 reduce-scatter.11
  452.8 106.7 reduce-scatter.9
  571.7 58.8 reduce-scatter.13
